TPU v7x, 128 devices: a whole 4x4x4 slice. The times are simulated.
128 devices in a mesh: half: 2 (over core), row: 8 (over z_hi, x), col: 8 (over y, z_lo).
Axes of the slice: x: 4, y: 4, z: 4 (z_hi: 2, z_lo: 2; z = z_hi * 2 + z_lo), core: 2. Of those that a mesh axis runs over, the one named last changes fastest.
Arguments:
- child_diag: float32 [2, 512, 512], P('half'), as said below
- child_panel: float32 [2, 16, 8, 128, 512], P('half', None, 'row'), may hold values from -18 to 18
- child_window: float32 [2, 16, 8, 128, 8, 8, 128], P('half', None, 'row', None, None, 'col'), may hold values from -6 to 6
- parent_diag: float32 [512, 512], replicated
- parent_lead_panel: float32 [24, 8, 2, 8, 8, 512], P(None, 'row', 'half', 'col'), may hold values from -24 to 24
- index_maps: int32 [2, 128], replicated, may hold values from 0 to 191, as said below
Outputs:
- parent_front: float32 [24, 8, 128, 4, 2, 8, 128], P(None, 'row', None, None, 'half', 'col')
- parent_factor: float32 [24, 8, 2, 8, 8, 512], P(None, 'row', 'half', 'col')
- parent_pivot: float32 [512, 512], replicated
Inputs may be any that keep to these rules, and one draw needn't show every extreme that they name: child_diag and parent_diag are symmetric and positive definite. For each child k and each group a, the entries index_maps[k, a * 16 + u] with 0 <= u < 16 equal q * 16 + ((u + s) mod 16) for a group target q and a turn s fixed within the group; groups a < 4 have q = a, later groups have distinct q that rise with a; over the 8 groups of a child the turns s, taken modulo 8, are all different; for each child some group a < 4 has a turn divisible by 8, and another group a < 4 has a turn that leaves 1 modulo 8.
All inputs are finite; a program needn't handle non-finite values.
Results may differ from a plain program's by a relative error of at most 0.0001.
Values sent between devices are 32-bit elements; how exact they have to be, the bound alone decides.
No kernel may reach another device: no remote copies, remote signals or barrier semaphores. Data moves between devices by JAX's collectives and lax.ppermute only.
A program may use at most 192 MiB of HBM per device.

v0:
```python
import jax
import jax.numpy as jnp
from jax import lax
from jax.sharding import PartitionSpec as P

BLOCK_EXTENT = 128
PB = 4
SB = 128
RB = 192
WB = 64


def from_root(shard, axis, root):
    mine = lax.axis_index(axis) == root
    return lax.psum(jnp.where(mine, shard, jnp.zeros_like(shard)), axis)


def pick_ranked(owners, values, wanted, slot_count, missing):
    matches = owners[..., None, :] == wanted[:, None]
    ranking = jnp.cumsum(matches.astype(jnp.int32), axis=-1) - 1
    slot_ids = jnp.arange(slot_count, dtype=jnp.int32)
    chosen = matches[..., None, :] & (ranking[..., None, :] == slot_ids[:, None])
    present = jnp.any(chosen, axis=-1)
    picked = jnp.sum(jnp.where(chosen, values[..., None, None, :], 0), axis=-1)
    return jnp.where(present, picked, missing)


def _dot_t(x, y):
    return lax.dot_general(x, y, (((1,), (1,)), ((), ())), precision=lax.Precision.HIGHEST)


def _dot(x, y):
    return jnp.dot(x, y, precision=lax.Precision.HIGHEST)


def factor_and_inverse(spd, leaf):
    order = spd.shape[0]
    blocks = order // leaf
    work = spd
    columns = []
    inverses = []
    eye = jnp.eye(leaf, dtype=spd.dtype)
    for k in range(blocks):
        low = jnp.linalg.cholesky(work[:leaf, :leaf])
        inv = lax.linalg.triangular_solve(low, eye, left_side=True, lower=True)
        inverses.append(inv)
        if k < blocks - 1:
            below = _dot_t(work[leaf:, :leaf], inv)
            work = work[leaf:, leaf:] - _dot_t(below, below)
            columns.append(jnp.concatenate([low, below], axis=0))
        else:
            columns.append(low)
    lower = jnp.concatenate(
        [jnp.pad(c, ((order - c.shape[0], 0), (0, 0))) for c in columns], axis=1
    )
    size = leaf
    while len(inverses) > 1:
        merged = []
        for t in range(0, len(inverses), 2):
            start = t * size
            first, second = (inverses[t], inverses[t + 1])
            coupling = lower[start + size : start + 2 * size, start : start + size]
            corner = -_dot(second, _dot(coupling, first))
            top = jnp.concatenate([first, jnp.zeros_like(first)], axis=1)
            bottom = jnp.concatenate([corner, second], axis=1)
            merged.append(jnp.concatenate([top, bottom], axis=0))
        inverses = merged
        size *= 2
    return (lower, inverses[0])


def per_device(child_diag, child_panel, child_window, parent_diag, parent_lead_panel, index_maps):
    highest = lax.Precision.HIGHEST
    row_size = lax.axis_size("row")
    col_size = lax.axis_size("col")
    half_id = lax.axis_index("half")
    row_id = lax.axis_index("row")
    col_id = lax.axis_index("col")
    panel_width = PB * BLOCK_EXTENT
    group_size = 2 * row_size
    row_local = SB // row_size
    col_local = WB // row_size
    parent_row_blocks = RB // row_size
    parent_cols = WB // group_size
    per_row = 2 * (SB // group_size) // row_size
    per_col = (WB // group_size + row_size - 1) // row_size
    transpose_perm = [
        (i * col_size + j, j * row_size + i)
        for i in range(row_size)
        for j in range(col_size)
        if i != j
    ]
    on_diagonal = row_id == col_id
    child_lead = child_panel[0, :col_local, 0]
    child_col_rows = jnp.where(
        on_diagonal, child_lead, lax.ppermute(child_lead, ("row", "col"), transpose_perm)
    )
    sub_rows = parent_lead_panel.shape[4]
    own_rows = parent_lead_panel.reshape(-1, panel_width)
    gathered = lax.all_gather(
        parent_lead_panel.reshape(parent_row_blocks, sub_rows, panel_width),
        ("half", "col"),
        axis=1,
        tiled=True,
    )
    leading_parent = parent_lead_panel.reshape(parent_row_blocks, sub_rows, panel_width)[
        : 2 * parent_cols
    ]
    transposed = jnp.where(
        on_diagonal, leading_parent, lax.ppermute(leading_parent, ("row", "col"), transpose_perm)
    )
    column_blocks = lax.all_gather(transposed, ("half", "row"), axis=1, tiled=True)
    parent_col_rows = lax.dynamic_index_in_dim(
        column_blocks.reshape(parent_cols, 2, BLOCK_EXTENT, panel_width),
        half_id,
        axis=1,
        keepdims=False,
    )
    child_low, child_inv = factor_and_inverse(child_diag[0], BLOCK_EXTENT)
    child_rows = child_panel.reshape(-1, panel_width)
    dims = (((1,), (1,)), ((), ()))
    high = lax.Precision.HIGH
    child_factor = lax.dot_general(child_rows, child_inv, dims, precision=high)
    child_columns = lax.dot_general(
        child_col_rows.reshape(-1, panel_width), child_inv, dims, precision=high
    )
    schur_part = child_window.reshape(
        row_local * BLOCK_EXTENT, col_local * BLOCK_EXTENT
    ) - lax.dot_general(child_factor, child_columns, dims, precision=high)
    child_map = lax.dynamic_index_in_dim(index_maps, half_id, axis=0, keepdims=False)
    my_rows = lax.dynamic_index_in_dim(
        child_map.reshape(row_local, row_size), row_id, axis=1, keepdims=False
    )
    my_cols = lax.dynamic_index_in_dim(
        child_map[:WB].reshape(col_local, row_size), col_id, axis=1, keepdims=False
    )
    local_rows = jnp.arange(row_local, dtype=jnp.int32)
    local_cols = jnp.arange(col_local, dtype=jnp.int32)
    send_rows = pick_ranked(
        my_rows % row_size, local_rows, jnp.arange(row_size, dtype=jnp.int32), per_row, row_local
    )
    send_cols = pick_ranked(
        my_cols % group_size,
        local_cols,
        jnp.arange(group_size, dtype=jnp.int32),
        per_col,
        col_local,
    )
    all_rows = index_maps.reshape(2, row_local, row_size).transpose(0, 2, 1)
    row_target = pick_ranked(
        all_rows % row_size, all_rows // row_size, row_id[None], per_row, parent_row_blocks
    )[:, :, 0, :]
    all_cols = index_maps[:, :WB].reshape(2, col_local, row_size).transpose(0, 2, 1)
    col_target = pick_ranked(
        all_cols % group_size,
        all_cols // group_size,
        (half_id * row_size + col_id)[None],
        per_col,
        parent_cols,
    )[:, :, 0, :]
    schur_blocks = schur_part.reshape(row_local, BLOCK_EXTENT, col_local, BLOCK_EXTENT)
    send_row_index = jnp.minimum(send_rows, row_local - 1)[None, :, None, :, None]
    send_col_index = jnp.minimum(send_cols, col_local - 1).reshape(2, row_size, per_col)[
        :, None, :, None, :
    ]
    outgoing = schur_blocks[send_row_index, :, send_col_index, :]
    outgoing, gathered, parent_col_rows, parent_diag = lax.optimization_barrier(
        (outgoing, gathered, parent_col_rows, parent_diag)
    )
    pivot_lower_factor, parent_inv = factor_and_inverse(parent_diag, BLOCK_EXTENT)
    solved = lax.dot_general(own_rows, parent_inv, dims, precision=highest)
    parent_factor = solved.reshape(parent_lead_panel.shape)
    row_factor = lax.dot_general(
        gathered.reshape(-1, panel_width), parent_inv, dims, precision=highest
    )
    column_factor = lax.dot_general(
        parent_col_rows.reshape(-1, panel_width), parent_inv, dims, precision=highest
    )
    update = lax.dot_general(row_factor, column_factor, dims, precision=highest)
    arrived = lax.all_to_all(
        outgoing.reshape(-1, per_row * per_col, BLOCK_EXTENT, BLOCK_EXTENT),
        ("half", "row", "col"),
        split_axis=0,
        concat_axis=0,
        tiled=True,
    )
    slot_shape = (2, row_size, row_size, per_row, per_col)
    slot_rows = jnp.broadcast_to(row_target[:, :, None, :, None], slot_shape).reshape(2, -1)
    slot_cols = jnp.broadcast_to(col_target[:, None, :, None, :], slot_shape).reshape(2, -1)
    slots = slot_rows.shape[1]
    match = (
        slot_rows[:, None, None, :]
        == jnp.arange(parent_row_blocks, dtype=jnp.int32)[None, :, None, None]
    ) & (
        slot_cols[:, None, None, :] == jnp.arange(parent_cols, dtype=jnp.int32)[None, None, :, None]
    )
    slot_of = jnp.sum(jnp.where(match, jnp.arange(slots, dtype=jnp.int32), 0), axis=-1)
    present = jnp.any(match, axis=-1)
    flat_arrived = arrived.reshape(2 * slots, BLOCK_EXTENT, BLOCK_EXTENT)
    block_shape = (parent_row_blocks, parent_cols, BLOCK_EXTENT, BLOCK_EXTENT)
    first = jnp.take(flat_arrived, slot_of[0].reshape(-1), axis=0, mode="clip")
    second = jnp.take(flat_arrived, slot_of[1].reshape(-1) + slots, axis=0, mode="clip")
    assembled = jnp.where(
        present[0, :, :, None, None], first.reshape(block_shape), 0.0
    ) + jnp.where(present[1, :, :, None, None], second.reshape(block_shape), 0.0)
    updated = assembled.transpose(0, 2, 1, 3) - update.reshape(
        parent_row_blocks, BLOCK_EXTENT, parent_cols, BLOCK_EXTENT
    )
    return (
        updated.reshape(parent_row_blocks, 1, BLOCK_EXTENT, parent_cols, 1, 1, BLOCK_EXTENT),
        parent_factor,
        pivot_lower_factor,
    )


def solution(mesh):
    in_specs = (
        P("half", None, None),
        P("half", None, "row", None, None),
        P("half", None, "row", None, None, "col", None),
        P(),
        P(None, "row", "half", "col", None, None),
        P(),
    )
    out_specs = (
        P(None, "row", None, None, "half", "col", None),
        P(None, "row", "half", "col", None, None),
        P(),
    )
    return jax.shard_map(
        per_device, mesh=mesh, in_specs=in_specs, out_specs=out_specs, check_vma=False
    )
```

profile of v0, /device:TPU:10, one launch (start us, length us, event | category | flops | bytes accessed | tf_op | source)
XLA Modules:
  0.0 529.1 jit_solution(2536918463805677017)
XLA Ops:
  8.2 4.6 collective-permute-start.1
  12.9 7.8 %collective-permute-done.1 = f32[8,8,512]{2,1,0:T(8,128)S(1)} collective-permute-done((f32[8,8,512]{2,1,0:T(8,128)S(1)}, f32[8,8,512]{2,1,0:T(8,128)S(1)}, u32[]{:S(2)}, u32[]{:S(2)}) %collective-permute-start.1) | collective-permute-done | bytes 131104 | tf_op jit(solution)/shard_map/ppermute | solution.py:110
  20.7 1.6 broadcast_select_fusion.1
  23.1 3.1 slice_bitcast_fusion
  26.2 4.7 collective-permute-start
  31.4 1.3 fusion.112
  35.1 11.7 %cholesky.134 = f32[128,128]{1,0:T(8,128)S(1)} custom-call(f32[128,128]{1,0:T(8,128)S(1)} %fusion.69), custom_call_target="Cholesky" | custom-call | tf_op jit(solution)/shard_map/jit(cholesky)/cholesky | solution.py:44
  48.1 9.8 %custom-call.14 = f32[1,128,128]{1,2,0:T(8,128)S(1)} custom-call(f32[1,128,128]{2,1,0:T(8,128)S(1)} %get-tuple-element.45), custom_call_target="InvertDiagBlocksLowerTriangular" | custom-call | tf_op jit(solution)/shard_map/triangular_solve/custom-call.0 | solution.py:45
  59.5 11.7 %cholesky.145 = f32[128,128]{1,0:T(8,128)S(1)} custom-call(f32[128,128]{1,0:T(8,128)S(1)} %fusion.67), custom_call_target="Cholesky" | custom-call | tf_op jit(solution)/shard_map/jit(cholesky)/cholesky | solution.py:44
  72.5 9.9 %custom-call.15 = f32[1,128,128]{1,2,0:T(8,128)S(1)} custom-call(f32[1,128,128]{2,1,0:T(8,128)S(1)} %get-tuple-element.43), custom_call_target="InvertDiagBlocksLowerTriangular" | custom-call | tf_op jit(solution)/shard_map/triangular_solve/custom-call.0 | solution.py:45
  83.9 11.7 %cholesky.156 = f32[128,128]{1,0:T(8,128)S(1)} custom-call(f32[128,128]{1,0:T(8,128)S(1)} %fusion.65), custom_call_target="Cholesky" | custom-call | tf_op jit(solution)/shard_map/jit(cholesky)/cholesky | solution.py:44
  96.9 9.8 %custom-call.16 = f32[1,128,128]{1,2,0:T(8,128)S(1)} custom-call(f32[1,128,128]{2,1,0:T(8,128)S(1)} %fusion.44), custom_call_target="InvertDiagBlocksLowerTriangular" | custom-call | tf_op jit(solution)/shard_map/triangular_solve/custom-call.0 | solution.py:45
  107.7 11.9 %cholesky.167 = f32[128,128]{1,0:T(8,128)S(1)} custom-call(f32[128,128]{1,0:T(8,128)S(1)} %fusion.63), custom_call_target="Cholesky" | custom-call | tf_op jit(solution)/shard_map/jit(cholesky)/cholesky | solution.py:44
  121.0 9.8 %custom-call.17 = f32[1,128,128]{1,2,0:T(8,128)S(1)} custom-call(f32[1,128,128]{2,1,0:T(8,128)S(1)} %fusion.45), custom_call_target="InvertDiagBlocksLowerTriangular" | custom-call | tf_op jit(solution)/shard_map/triangular_solve/custom-call.0 | solution.py:45
  133.4 5.9 %fusion.3 = f32[512,2048]{1,0:T(8,128)S(1)} fusion(f32[2048,512]{1,0:T(8,128)} %bitcast.242, f32[256,256]{1,0:T(8,128)S(1)} %select_maximum_fusion.9, f32[128,128]{1,0:T(8,128)S(1)} %copy.131, f32[128,128]{1,0:T(8,128)S(1)} %convolution_negate_fusion.4, f32[128,256]{1,0:T(8,128)S(1)} %concatenate.86, f32[256,256]{1,0:T(8,128)S(1)} %convolution_negate_fusion.1), kind=kOutput, calls=%fused_computation.29 | convolution fusion | flops 3222798336 | bytes 9175040 | tf_op jit(solution)/shard_map/dot_general | solution.py:123
  139.4 2.2 broadcast_select_fusion
  141.6 1.9 fusion.2
  143.5 15.2 %fusion = f32[256,8,8,128]{3,1,2,0:T(8,128)S(1)} fusion(f32[256,8,8,128]{3,2,1,0:T(8,128)S(1)} %bitcast.246, f32[512,2048]{1,0:T(8,128)S(1)} %fusion.3, f32[1024,512]{1,0:T(8,128)S(1)} %fusion.2), kind=kOutput, calls=%fused_computation.4 | convolution fusion | flops 6444548096 | bytes 23068672 | tf_op jit(solution)/shard_map/dot_general | solution.py:129
  158.7 2.1 copy.171
  160.8 4.7 copy.137
  165.5 16.2 %gather_fusion = f32[256,128,128]{2,1,0:T(8,128)} fusion(f32[16,128,8,128]{3,1,2,0:T(8,128)} %copy.137, s32[256]{0:T(256)S(1)} %reshape.466), kind=kCustom, calls=%fused_computation | custom fusion | bytes 33556480 | tf_op jit(solution)/shard_map/gather | solution.py:166
  181.7 2.3 dynamic-slice_bitcast_fusion
  184.0 18.0 %all-gather.6.cloned.1.call-done = f32[24,1,1,1,128,512]{5,4,3,2,1,0:T(8,128)} async-done(((f32[24,1,1,1,8,512]{5,4,3,2,1,0:T(8,128)}), f32[24,1,1,1,128,512]{5,4,3,2,1,0:T(8,128)}) %all-gather.6.cloned.1.call-update) | async-done | bytes 6291472 | tf_op jit(solution)/shard_map/all_gather | solution.py:100
  202.0 9.6 %all-to-all-start = ((f32[128,2,128,128]{3,2,1,0:T(8,128)}), f32[128,2,128,128]{3,2,1,0:T(8,128)}, u32[]{:S(2)}, u32[]{:S(2)}) async-start(f32[128,2,128,128]{3,2,1,0:T(8,128)} %bitcast.238), calls=%async_computation | async-start | bytes 33554432 | tf_op jit(solution)/shard_map/all_to_all | solution.py:180
  215.1 11.7 %cholesky.178 = f32[128,128]{1,0:T(8,128)S(1)} custom-call(f32[128,128]{1,0:T(8,128)S(1)} %fusion.61), custom_call_target="Cholesky" | custom-call | tf_op jit(solution)/shard_map/jit(cholesky)/cholesky | solution.py:44
  228.1 9.8 %custom-call.18 = f32[1,128,128]{1,2,0:T(8,128)S(1)} custom-call(f32[1,128,128]{2,1,0:T(8,128)S(1)} %get-tuple-element.37), custom_call_target="InvertDiagBlocksLowerTriangular" | custom-call | tf_op jit(solution)/shard_map/triangular_solve/custom-call.0 | solution.py:45
  238.2 1.3 fusion.37
  241.9 11.9 %cholesky.189 = f32[128,128]{1,0:T(8,128)S(1)} custom-call(f32[128,128]{1,0:T(8,128)S(1)} %fusion.59), custom_call_target="Cholesky" | custom-call | tf_op jit(solution)/shard_map/jit(cholesky)/cholesky | solution.py:44
  255.1 9.8 %custom-call.19 = f32[1,128,128]{1,2,0:T(8,128)S(1)} custom-call(f32[1,128,128]{2,1,0:T(8,128)S(1)} %get-tuple-element.35), custom_call_target="InvertDiagBlocksLowerTriangular" | custom-call | tf_op jit(solution)/shard_map/triangular_solve/custom-call.0 | solution.py:45
  265.3 1.3 fusion.39
  266.6 1.3 convolution_subtract_fusion.2
  268.1 11.7 %cholesky.200 = f32[128,128]{1,0:T(8,128)S(1)} custom-call(f32[128,128]{1,0:T(8,128)S(1)} %fusion.57), custom_call_target="Cholesky" | custom-call | tf_op jit(solution)/shard_map/jit(cholesky)/cholesky | solution.py:44
  280.5 1.3 select_bitcast_fusion.1
  281.8 9.8 %custom-call.20 = f32[1,128,128]{1,2,0:T(8,128)S(1)} custom-call(f32[1,128,128]{2,1,0:T(8,128)S(1)} %get-tuple-element.33), custom_call_target="InvertDiagBlocksLowerTriangular" | custom-call | tf_op jit(solution)/shard_map/triangular_solve/custom-call.0 | solution.py:45
  292.6 11.9 %cholesky.211 = f32[128,128]{1,0:T(8,128)S(1)} custom-call(f32[128,128]{1,0:T(8,128)S(1)} %fusion.55), custom_call_target="Cholesky" | custom-call | tf_op jit(solution)/shard_map/jit(cholesky)/cholesky | solution.py:44
  305.2 1.3 select_bitcast_fusion
  306.4 9.8 %custom-call.21 = f32[1,128,128]{1,2,0:T(8,128)S(1)} custom-call(f32[1,128,128]{2,1,0:T(8,128)S(1)} %get-tuple-element.31), custom_call_target="InvertDiagBlocksLowerTriangular" | custom-call | tf_op jit(solution)/shard_map/triangular_solve/custom-call.0 | solution.py:45
  317.2 1.9 select_maximum_fusion.5
  320.4 3.1 fusion.105
  323.5 11.5 %fusion.106 = f32[3072,512]{1,0:T(8,128)S(1)} fusion(f32[3072,512]{1,0:T(8,128)S(1)} %bitcast.249, f32[256,256]{1,0:T(8,128)S(1)} %select_maximum_fusion.7, f32[128,128]{1,0:T(8,128)S(1)} %copy.153, f32[128,128]{1,0:T(8,128)S(1)} %convolution_negate_fusion.2, f32[128,256]{1,0:T(8,128)S(1)} %concatenate.99, f32[256,256]{1,0:T(8,128)S(1)} %convolution_negate_fusion), kind=kOutput, calls=%fused_computation.239 | convolution fusion | flops 9665249280 | bytes 13369344 | tf_op jit(solution)/shard_map/dot_general | solution.py:173
  335.0 12.1 %fusion.118 = f32[3072,512]{1,0:T(8,128)} fusion(f32[3072,512]{1,0:T(8,128)S(1)} %fusion.106, f32[512,512]{1,0:T(8,128)S(1)} %fusion.105), kind=kOutput, calls=%fused_computation.246 | convolution fusion | flops 9663676416 | bytes 13631488 | tf_op jit(solution)/shard_map/dot_general | solution.py:179
  347.1 7.8 %reshape.446 = f32[24,128,4,128]{3,2,1,0:T(4,128)} reshape(f32[3072,512]{1,0:T(8,128)} %fusion.118) | data formatting | bytes 12582912 | tf_op jit(solution)/shard_map/reshape | solution.py:206
  355.9 1.8 convolution_bitcast_fusion
  357.7 130.7 %all-to-all-done = f32[128,2,128,128]{3,2,1,0:T(8,128)} async-done(((f32[128,2,128,128]{3,2,1,0:T(8,128)}), f32[128,2,128,128]{3,2,1,0:T(8,128)}, u32[]{:S(2)}, u32[]{:S(2)}) %all-to-all-start) | async-done | bytes 16777248 | tf_op jit(solution)/shard_map/all_to_all | solution.py:180
  488.4 9.4 %gather_fusion.2 = f32[96,128,128]{2,1,0:T(8,128)} fusion(f32[256,128,128]{2,1,0:T(8,128)} %bitcast.28, s32[1024]{0:T(1024)S(1)} %pad_clamp_fusion), kind=kCustom, calls=%fused_computation.2 | custom fusion | bytes 12583296 | tf_op jit(solution)/shard_map/jit(_take)/gather | solution.py:202
  497.8 9.4 %gather_fusion.1 = f32[96,128,128]{2,1,0:T(8,128)} fusion(f32[256,128,128]{2,1,0:T(8,128)} %bitcast.28, s32[1024]{0:T(1024)S(1)} %pad_clamp_fusion.1), kind=kCustom, calls=%fused_computation.1 | custom fusion | bytes 12583296 | tf_op jit(solution)/shard_map/jit(_take)/gather | solution.py:201
  507.2 7.4 %fusion.1 = f32[24,1,128,4,1,1,128]{6,2,3,0,5,4,1:T(8,128)S(1)} fusion(f32[24,128,4,128]{3,2,1,0:T(4,128)} %reshape.446, f32[24,4,128,128]{3,2,1,0:T(8,128)} %bitcast.240, f32[24,4,128,128]{3,2,1,0:T(8,128)} %bitcast.241, pred[24,4]{1,0:T(8,128)(4,1)S(1)} %copy.139, pred[24,4]{1,0:T(8,128)(4,1)S(1)} %copy.119), kind=kLoop, calls=%fused_computation.6 | loop fusion | flops 6291456 | bytes 25166016 | tf_op jit(solution)/shard_map/reshape | solution.py:210
  514.6 7.5 %copy.156 = f32[24,1,128,4,1,1,128]{6,5,4,3,2,1,0:T(1,128)} copy(f32[24,1,128,4,1,1,128]{6,2,3,0,5,4,1:T(8,128)S(1)} %fusion.1) | data formatting | bytes 12582912
  (185 shorter events, 30.8 us)
Async XLA Ops:
  7.2 27.4 %copy-start.6 = (f32[1,512,512]{2,1,0:T(8,128)S(1)}, f32[1,512,512]{2,1,0:T(8,128)}, u32[]{:S(2)}) copy-start(f32[1,512,512]{2,1,0:T(8,128)} %param.9) | copy-start | bytes 3145732
  7.2 174.5 %all-gather.4.cloned.1.call-start = ((), (), s32[]{:S(2)}) async-start(), calls=%async_computation.1 | async-start | bytes 2228224 | tf_op jit(solution)/shard_map/all_gather | solution.py:112
  8.2 12.5 %collective-permute-start.1 = (f32[8,8,512]{2,1,0:T(8,128)S(1)}, f32[8,8,512]{2,1,0:T(8,128)S(1)}, u32[]{:S(2)}, u32[]{:S(2)}) collective-permute-start(f32[8,8,512]{2,1,0:T(8,128)S(1)} %slice_bitcast_fusion.1), channel_id=1, source_target_pairs={{1,8},{2,16},{3,24},{4,32},{5,40},{6,48},{7,56},{8,1},{10,17},{11,... | collective-permute-start | bytes 393224 | tf_op jit(solution)/shard_map/ppermute | solution.py:110
  22.3 179.6 %all-gather.6.cloned.1.call-start = ((), (), s32[]{:S(2)}) async-start(), calls=%async_computation.2 | async-start | bytes 6684672 | tf_op jit(solution)/shard_map/all_gather | solution.py:100
  26.2 113.2 %collective-permute-start = (f32[8,128,512]{2,1,0:T(8,128)}, f32[8,128,512]{2,1,0:T(8,128)}, u32[]{:S(2)}, u32[]{:S(2)}) collective-permute-start(f32[8,128,512]{2,1,0:T(8,128)} %slice_bitcast_fusion), channel_id=1, source_target_pairs={{1,8},{2,16},{3,24},{4,32},{5,40},{6,48},{7,56},{8,1},{10,17},{11,... | collective-permute-start | bytes 6291464 | tf_op jit(solution)/shard_map/ppermute | solution.py:96
  131.3 8.1 %copy-start = (f32[1,16,1,128,512]{4,3,2,1,0:T(8,128)S(1)}, f32[1,16,1,128,512]{4,3,2,1,0:T(8,128)}, u32[]{:S(2)}) copy-start(f32[1,16,1,128,512]{4,3,2,1,0:T(8,128)} %param.10) | copy-start | bytes 12582916
  133.4 10.1 %slice-start = ((s8[8388608]{0:T(1024)(128)(4,1)}), s8[4194304]{0:T(1024)(128)(4,1)S(1)}, s32[]{:S(2)}) async-start(s8[8388608]{0:T(1024)(128)(4,1)} %bitcast.244), calls=%async_computation.3 | async-start | bytes 8388608
  139.3 4.1 slice-start.1
  202.0 9.6 %copy-start.9 = (s32[2,128]{1,0:T(2,128)S(1)}, s32[2,128]{1,0:T(2,128)}, u32[]{:S(2)}) copy-start(s32[2,128]{1,0:T(2,128)} %param.14) | copy-start | bytes 3076
  202.0 12.6 %copy-start.2 = (f32[512,512]{1,0:T(8,128)S(1)}, f32[512,512]{1,0:T(8,128)}, u32[]{:S(2)}) copy-start(f32[512,512]{1,0:T(8,128)} %param.12) | copy-start | bytes 3145732
  202.0 286.4 %all-to-all-start = ((f32[128,2,128,128]{3,2,1,0:T(8,128)}), f32[128,2,128,128]{3,2,1,0:T(8,128)}, u32[]{:S(2)}, u32[]{:S(2)}) async-start(f32[128,2,128,128]{3,2,1,0:T(8,128)} %bitcast.238), calls=%async_computation | async-start | bytes 33554432 | tf_op jit(solution)/shard_map/all_to_all | solution.py:180
  215.0 108.5 %slice-start.2 = ((s8[6291456]{0:T(1024)(128)(4,1)}), s8[2097152]{0:T(1024)(128)(4,1)S(1)}, s32[]{:S(2)}) async-start(s8[6291456]{0:T(1024)(128)(4,1)} %bitcast.247), calls=%async_computation.5 | async-start | bytes 4194304
  240.2 0.8 copy-start.1
  316.6 6.9 %slice-start.3 = ((s8[6291456]{0:T(1024)(128)(4,1)}), s8[4194304]{0:T(1024)(128)(4,1)S(1)}, s32[]{:S(2)}) async-start(s8[6291456]{0:T(1024)(128)(4,1)} %bitcast.247), calls=%async_computation.6 | async-start | bytes 8388608
  317.2 17.8 %copy-start.4 = (f32[256,256]{1,0:T(8,128)}, f32[256,256]{1,0:T(8,128)S(1)}, u32[]{:S(2)}) copy-start(f32[256,256]{1,0:T(8,128)S(1)} %select_maximum_fusion.7) | copy-start | bytes 786436
  347.1 7.8 %copy-start.7 = (f32[512,128]{1,0:T(8,128)S(1)}, f32[512,128]{1,0:T(8,128)}, u32[]{:S(2)}) copy-start(f32[512,128]{1,0:T(8,128)} %get-tuple-element.55) | copy-start | bytes 786436
  347.1 7.8 %copy-start.8 = (f32[128,128]{1,0:T(8,128)S(1)}, f32[128,128]{1,0:T(8,128)}, u32[]{:S(2)}) copy-start(f32[128,128]{1,0:T(8,128)} %get-tuple-element.32) | copy-start | bytes 196612
  347.1 8.9 %copy-start.3 = (f32[24,1,1,1,8,512]{5,4,3,2,1,0:T(8,128)S(1)}, f32[24,1,1,1,8,512]{5,4,3,2,1,0:T(8,128)}, u32[]{:S(2)}) copy-start(f32[24,1,1,1,8,512]{5,4,3,2,1,0:T(8,128)} %param.13) | copy-start | bytes 1179652
  347.1 8.9 %copy-start.5 = (f32[256,256]{1,0:T(8,128)S(1)}, f32[256,256]{1,0:T(8,128)}, u32[]{:S(2)}) copy-start(f32[256,256]{1,0:T(8,128)} %copy-done.4) | copy-start | bytes 786436
Sparse Core Ops, SparseCore 0:
  22.4 136.6 all-gather.3
  160.9 41.0 all-gather.5
where the time goes:
time: 539 us; the launch traced here: 529 us
  other arithmetic  202 us (37%)
  waiting for transfers between devices  157 us (29%)
  local copies, waits for them, and re-layouts  70.5 us (13%)
  matrix products  64.7 us (12%)
  starting transfers between devices  19 us (4%)
  between operations  15.3 us (3%)
    all_to_all x1, waiting for transfers between devices, per_device(): lax.all_to_all(outgoing.reshape(-1, per_row * per_col, BLOCK_EXTENT, BLOC...  131 us
    another operation x24, other arithmetic, factor_and_inverse(): low = jnp.linalg.cholesky(work[:leaf, :leaf])  99.7 us
    another operation x16, other arithmetic, factor_and_inverse(): inv = lax.linalg.triangular_solve(low, eye, left_side=True, lower=True)  85.1 us
    all_gather x1, waiting for transfers between devices, per_device(): lax.all_gather(parent_lead_panel.reshape(parent_row_blocks, sub_rows, pan...  18 us
    gather x1, local copies, waits for them, and re-layouts, per_device(): outgoing = schur_blocks[send_row_index, :, send_col_index, :]  16.2 us
    dot_general x1, matrix products, per_device(): lax.dot_general(child_factor, child_columns, dims, precision=high)  15.2 us
    dot_general x1, matrix products, per_device(): update = lax.dot_general(row_factor, column_factor, dims, precision=highest)  12.1 us
    dot_general x1, matrix products, per_device(): lax.dot_general(gathered.reshape(-1, panel_width), parent_inv, dims, prec...  11.5 us
  transfers between devices with their start and end apart: 5, of which 3 were waited for; matrix products, arithmetic and copies ran while one was open for 57% of the time, Pallas kernels for 0%

commit v1 on v0

--- a/solution.py
+++ b/solution.py
@@ -97,11 +97,17 @@
     )
     sub_rows = parent_lead_panel.shape[4]
     own_rows = parent_lead_panel.reshape(-1, panel_width)
-    gathered = lax.all_gather(
-        parent_lead_panel.reshape(parent_row_blocks, sub_rows, panel_width),
-        ("half", "col"),
+    gathered = jnp.concatenate(
+        lax.all_to_all(
+            jnp.stack(
+                [parent_lead_panel.reshape(parent_row_blocks, sub_rows, panel_width)]
+                * lax.axis_size(("half", "col"))
+            ),
+            ("half", "col"),
+            0,
+            0,
+        ),
         axis=1,
-        tiled=True,
     )
     leading_parent = parent_lead_panel.reshape(parent_row_blocks, sub_rows, panel_width)[
         : 2 * parent_cols

time: 539 us -> 553 us (1.026)
  starting transfers between devices: 19 us -> 40.6 us
  waiting for transfers between devices: 157 us -> 139 us
  local copies, waits for them, and re-layouts: 70.5 us -> 80.6 us
    all_gather x1 -> x0, waiting for transfers between devices: 18 us -> none  [per_device(): lax.all_gather(parent_lead_panel.reshape(parent_row_blocks, sub_rows, pan...]
    all_to_all x1, starting transfers between devices: 9.58 us -> 22.5 us  [per_device(): lax.all_to_all(outgoing.reshape(-1, per_row * per_col, BLOCK_EXTENT, BLOC...]
    all_to_all x0 -> x1, starting transfers between devices: none -> 10.5 us  [per_device(): lax.all_to_all(jnp.stack([parent_lead_panel.reshape(parent_row_blocks, su...]
    all_gather x1, waiting for transfers between devices: 0.01 us -> 8.35 us  [per_device(): lax.all_gather(transposed, ('half', 'row'), axis=1, tiled=True)]
    ppermute x1, waiting for transfers between devices: 7.85 us -> 0.01 us  [per_device(): lax.ppermute(leading_parent, ('row', 'col'), transpose_perm)]
    all_to_all x0 -> x1, local copies, waits for them, and re-layouts: none -> 6.53 us  [per_device(): lax.all_to_all(jnp.stack([parent_lead_panel.reshape(parent_row_blocks, su...]
  transfers between devices with their start and end apart: 5 -> 5, of which waited for: 3 -> 2; matrix products, arithmetic and copies ran while one was open for 57% -> 56% of each run, Pallas kernels for 0% -> 0%
where the time goes in v1:
time: 553 us; the launch traced here: 543 us
  other arithmetic  202 us (37%)
  waiting for transfers between devices  139 us (25%)
  local copies, waits for them, and re-layouts  80.6 us (15%)
  matrix products  64.7 us (12%)
  starting transfers between devices  40.6 us (7%)
  between operations  15.3 us (3%)
    all_to_all x1, waiting for transfers between devices, per_device(): lax.all_to_all(outgoing.reshape(-1, per_row * per_col, BLOCK_EXTENT, BLOC...  131 us
    another operation x24, other arithmetic, factor_and_inverse(): low = jnp.linalg.cholesky(work[:leaf, :leaf])  99.6 us
    another operation x16, other arithmetic, factor_and_inverse(): inv = lax.linalg.triangular_solve(low, eye, left_side=True, lower=True)  85.1 us
    all_to_all x1, starting transfers between devices, per_device(): lax.all_to_all(outgoing.reshape(-1, per_row * per_col, BLOCK_EXTENT, BLOC...  22.5 us
    gather x1, local copies, waits for them, and re-layouts, per_device(): outgoing = schur_blocks[send_row_index, :, send_col_index, :]  16 us
    dot_general x1, matrix products, per_device(): lax.dot_general(child_factor, child_columns, dims, precision=high)  15.2 us
    dot_general x1, matrix products, per_device(): update = lax.dot_general(row_factor, column_factor, dims, precision=highest)  12.1 us
    dot_general x1, matrix products, per_device(): lax.dot_general(gathered.reshape(-1, panel_width), parent_inv, dims, prec...  11.5 us
  transfers between devices with their start and end apart: 5, of which 2 were waited for; matrix products, arithmetic and copies ran while one was open for 56% of the time, Pallas kernels for 0%

profile of v1, /device:TPU:10, one launch (start us, length us, event | category | flops | bytes accessed | tf_op | source)
XLA Modules:
  0.0 542.6 jit_solution(6667339026826774119)
XLA Ops:
  8.1 4.6 collective-permute-start.1
  12.7 3.1 slice_bitcast_fusion
  15.8 3.0 collective-permute-start
  18.8 4.5 stack.3
  23.4 10.5 %all-to-all-start = ((f32[16,24,8,512]{3,2,1,0:T(8,128)}), f32[16,24,8,512]{3,2,1,0:T(8,128)}, u32[]{:S(2)}, u32[]{:S(2)}) async-start(f32[16,24,8,512]{3,2,1,0:T(8,128)} %stack.3), calls=%async_computation | async-start | bytes 12582912 | tf_op jit(solution)/shard_map/all_to_all | solution.py:101
  36.3 11.7 %cholesky.134 = f32[128,128]{1,0:T(8,128)S(1)} custom-call(f32[128,128]{1,0:T(8,128)S(1)} %fusion.69), custom_call_target="Cholesky" | custom-call | tf_op jit(solution)/shard_map/jit(cholesky)/cholesky | solution.py:44
  49.4 9.8 %custom-call.14 = f32[1,128,128]{1,2,0:T(8,128)S(1)} custom-call(f32[1,128,128]{2,1,0:T(8,128)S(1)} %get-tuple-element.45), custom_call_target="InvertDiagBlocksLowerTriangular" | custom-call | tf_op jit(solution)/shard_map/triangular_solve/custom-call.0 | solution.py:45
  60.6 11.7 %cholesky.145 = f32[128,128]{1,0:T(8,128)S(1)} custom-call(f32[128,128]{1,0:T(8,128)S(1)} %fusion.67), custom_call_target="Cholesky" | custom-call | tf_op jit(solution)/shard_map/jit(cholesky)/cholesky | solution.py:44
  73.7 9.9 %custom-call.15 = f32[1,128,128]{1,2,0:T(8,128)S(1)} custom-call(f32[1,128,128]{2,1,0:T(8,128)S(1)} %get-tuple-element.43), custom_call_target="InvertDiagBlocksLowerTriangular" | custom-call | tf_op jit(solution)/shard_map/triangular_solve/custom-call.0 | solution.py:45
  84.8 11.7 %cholesky.156 = f32[128,128]{1,0:T(8,128)S(1)} custom-call(f32[128,128]{1,0:T(8,128)S(1)} %fusion.65), custom_call_target="Cholesky" | custom-call | tf_op jit(solution)/shard_map/jit(cholesky)/cholesky | solution.py:44
  97.9 9.8 %custom-call.16 = f32[1,128,128]{1,2,0:T(8,128)S(1)} custom-call(f32[1,128,128]{2,1,0:T(8,128)S(1)} %fusion.44), custom_call_target="InvertDiagBlocksLowerTriangular" | custom-call | tf_op jit(solution)/shard_map/triangular_solve/custom-call.0 | solution.py:45
  108.9 11.9 %cholesky.167 = f32[128,128]{1,0:T(8,128)S(1)} custom-call(f32[128,128]{1,0:T(8,128)S(1)} %fusion.63), custom_call_target="Cholesky" | custom-call | tf_op jit(solution)/shard_map/jit(cholesky)/cholesky | solution.py:44
  122.6 1.6 broadcast_select_fusion.1
  124.9 9.8 %custom-call.17 = f32[1,128,128]{1,2,0:T(8,128)S(1)} custom-call(f32[1,128,128]{2,1,0:T(8,128)S(1)} %fusion.45), custom_call_target="InvertDiagBlocksLowerTriangular" | custom-call | tf_op jit(solution)/shard_map/triangular_solve/custom-call.0 | solution.py:45
  137.3 5.9 %fusion.3 = f32[512,2048]{1,0:T(8,128)S(1)} fusion(f32[2048,512]{1,0:T(8,128)} %bitcast.250, f32[256,256]{1,0:T(8,128)S(1)} %select_maximum_fusion.9, f32[128,128]{1,0:T(8,128)S(1)} %copy.132, f32[128,128]{1,0:T(8,128)S(1)} %convolution_negate_fusion.4, f32[128,256]{1,0:T(8,128)S(1)} %concatenate.86, f32[256,256]{1,0:T(8,128)S(1)} %convolution_negate_fusion.1), kind=kOutput, calls=%fused_computation.30 | convolution fusion | flops 3222798336 | bytes 9175040 | tf_op jit(solution)/shard_map/dot_general | solution.py:129
  143.2 2.2 broadcast_select_fusion
  145.5 1.9 fusion.2
  147.4 15.2 %fusion = f32[256,8,8,128]{3,1,2,0:T(8,128)S(1)} fusion(f32[256,8,8,128]{3,2,1,0:T(8,128)S(1)} %bitcast.254, f32[512,2048]{1,0:T(8,128)S(1)} %fusion.3, f32[1024,512]{1,0:T(8,128)S(1)} %fusion.2), kind=kOutput, calls=%fused_computation.4 | convolution fusion | flops 6444548096 | bytes 23068672 | tf_op jit(solution)/shard_map/dot_general | solution.py:135
  162.6 2.1 copy.173
  164.6 4.7 copy.138
  169.3 16.0 %gather_fusion = f32[256,128,128]{2,1,0:T(8,128)} fusion(f32[16,128,8,128]{3,1,2,0:T(8,128)} %copy.138, s32[256]{0:T(256)S(1)} %reshape.472), kind=kCustom, calls=%fused_computation | custom fusion | bytes 33556480 | tf_op jit(solution)/shard_map/gather | solution.py:172
  185.4 8.3 %all-gather.2.cloned.1.call-done = f32[8,128,512]{2,1,0:T(8,128)} async-done(((f32[8,8,512]{2,1,0:T(8,128)}), f32[8,128,512]{2,1,0:T(8,128)}) %all-gather.2.cloned.1.call-update) | async-done | bytes 2097168 | tf_op jit(solution)/shard_map/all_gather | solution.py:118
  193.7 2.3 dynamic-slice_bitcast_fusion
  196.0 6.5 %copy.177 = f32[16,24,8,512]{3,2,0,1:T(8,128)} copy(f32[16,24,8,512]{3,2,1,0:T(8,128)} %all-to-all-done) | data formatting | bytes 12582912 | tf_op jit(solution)/shard_map/all_to_all | solution.py:101
  202.5 22.5 %all-to-all-start.1 = ((f32[128,2,128,128]{3,2,1,0:T(8,128)}), f32[128,2,128,128]{3,2,1,0:T(8,128)}, u32[]{:S(2)}, u32[]{:S(2)}) async-start(f32[128,2,128,128]{3,2,1,0:T(8,128)} %bitcast.243), calls=%async_computation.1 | async-start | bytes 33554432 | tf_op jit(solution)/shard_map/all_to_all | solution.py:186
  228.5 11.7 %cholesky.178 = f32[128,128]{1,0:T(8,128)S(1)} custom-call(f32[128,128]{1,0:T(8,128)S(1)} %fusion.61), custom_call_target="Cholesky" | custom-call | tf_op jit(solution)/shard_map/jit(cholesky)/cholesky | solution.py:44
  241.6 9.8 %custom-call.18 = f32[1,128,128]{1,2,0:T(8,128)S(1)} custom-call(f32[1,128,128]{2,1,0:T(8,128)S(1)} %get-tuple-element.37), custom_call_target="InvertDiagBlocksLowerTriangular" | custom-call | tf_op jit(solution)/shard_map/triangular_solve/custom-call.0 | solution.py:45
  255.4 11.9 %cholesky.189 = f32[128,128]{1,0:T(8,128)S(1)} custom-call(f32[128,128]{1,0:T(8,128)S(1)} %fusion.59), custom_call_target="Cholesky" | custom-call | tf_op jit(solution)/shard_map/jit(cholesky)/cholesky | solution.py:44
  268.6 9.8 %custom-call.19 = f32[1,128,128]{1,2,0:T(8,128)S(1)} custom-call(f32[1,128,128]{2,1,0:T(8,128)S(1)} %get-tuple-element.35), custom_call_target="InvertDiagBlocksLowerTriangular" | custom-call | tf_op jit(solution)/shard_map/triangular_solve/custom-call.0 | solution.py:45
  278.8 1.3 fusion.39
  280.1 1.3 convolution_subtract_fusion.2
  281.5 11.7 %cholesky.200 = f32[128,128]{1,0:T(8,128)S(1)} custom-call(f32[128,128]{1,0:T(8,128)S(1)} %fusion.57), custom_call_target="Cholesky" | custom-call | tf_op jit(solution)/shard_map/jit(cholesky)/cholesky | solution.py:44
  293.9 1.3 select_bitcast_fusion.1
  295.2 9.8 %custom-call.20 = f32[1,128,128]{1,2,0:T(8,128)S(1)} custom-call(f32[1,128,128]{2,1,0:T(8,128)S(1)} %get-tuple-element.33), custom_call_target="InvertDiagBlocksLowerTriangular" | custom-call | tf_op jit(solution)/shard_map/triangular_solve/custom-call.0 | solution.py:45
  306.0 11.9 %cholesky.211 = f32[128,128]{1,0:T(8,128)S(1)} custom-call(f32[128,128]{1,0:T(8,128)S(1)} %fusion.55), custom_call_target="Cholesky" | custom-call | tf_op jit(solution)/shard_map/jit(cholesky)/cholesky | solution.py:44
  318.6 1.3 select_bitcast_fusion
  319.9 9.8 %custom-call.21 = f32[1,128,128]{1,2,0:T(8,128)S(1)} custom-call(f32[1,128,128]{2,1,0:T(8,128)S(1)} %get-tuple-element.31), custom_call_target="InvertDiagBlocksLowerTriangular" | custom-call | tf_op jit(solution)/shard_map/triangular_solve/custom-call.0 | solution.py:45
  330.6 1.9 select_maximum_fusion.5
  333.8 3.1 fusion.105
  336.9 11.5 %fusion.106 = f32[3072,512]{1,0:T(8,128)S(1)} fusion(f32[3072,512]{1,0:T(8,128)S(1)} %bitcast.247, f32[256,256]{1,0:T(8,128)S(1)} %select_maximum_fusion.7, f32[128,128]{1,0:T(8,128)S(1)} %copy.155, f32[128,128]{1,0:T(8,128)S(1)} %convolution_negate_fusion.2, f32[128,256]{1,0:T(8,128)S(1)} %concatenate.99, f32[256,256]{1,0:T(8,128)S(1)} %convolution_negate_fusion), kind=kOutput, calls=%fused_computation.240 | convolution fusion | flops 9665249280 | bytes 13369344 | tf_op jit(solution)/shard_map/dot_general | solution.py:179
  348.4 12.1 %fusion.118 = f32[3072,512]{1,0:T(8,128)} fusion(f32[3072,512]{1,0:T(8,128)S(1)} %fusion.106, f32[512,512]{1,0:T(8,128)S(1)} %fusion.105), kind=kOutput, calls=%fused_computation.247 | convolution fusion | flops 9663676416 | bytes 13631488 | tf_op jit(solution)/shard_map/dot_general | solution.py:185
  360.5 7.8 %reshape.452 = f32[24,128,4,128]{3,2,1,0:T(4,128)} reshape(f32[3072,512]{1,0:T(8,128)} %fusion.118) | data formatting | bytes 12582912 | tf_op jit(solution)/shard_map/reshape | solution.py:212
  369.4 1.8 convolution_bitcast_fusion
  371.1 130.7 %all-to-all-done.1 = f32[128,2,128,128]{3,2,1,0:T(8,128)} async-done(((f32[128,2,128,128]{3,2,1,0:T(8,128)}), f32[128,2,128,128]{3,2,1,0:T(8,128)}, u32[]{:S(2)}, u32[]{:S(2)}) %all-to-all-start.1) | async-done | bytes 16777248 | tf_op jit(solution)/shard_map/all_to_all | solution.py:186
  501.9 9.4 %gather_fusion.2 = f32[96,128,128]{2,1,0:T(8,128)} fusion(f32[256,128,128]{2,1,0:T(8,128)} %bitcast.30, s32[1024]{0:T(1024)S(1)} %pad_clamp_fusion), kind=kCustom, calls=%fused_computation.2 | custom fusion | bytes 12583296 | tf_op jit(solution)/shard_map/jit(_take)/gather | solution.py:208
  511.3 9.4 %gather_fusion.1 = f32[96,128,128]{2,1,0:T(8,128)} fusion(f32[256,128,128]{2,1,0:T(8,128)} %bitcast.30, s32[1024]{0:T(1024)S(1)} %pad_clamp_fusion.1), kind=kCustom, calls=%fused_computation.1 | custom fusion | bytes 12583296 | tf_op jit(solution)/shard_map/jit(_take)/gather | solution.py:207
  520.7 7.4 %fusion.1 = f32[24,1,128,4,1,1,128]{6,2,3,0,5,4,1:T(8,128)S(1)} fusion(f32[24,128,4,128]{3,2,1,0:T(4,128)} %reshape.452, f32[24,4,128,128]{3,2,1,0:T(8,128)} %bitcast.248, f32[24,4,128,128]{3,2,1,0:T(8,128)} %bitcast.249, pred[24,4]{1,0:T(8,128)(4,1)S(1)} %copy.141, pred[24,4]{1,0:T(8,128)(4,1)S(1)} %copy.120), kind=kLoop, calls=%fused_computation.6 | loop fusion | flops 6291456 | bytes 25166016 | tf_op jit(solution)/shard_map/reshape | solution.py:216
  528.0 7.5 %copy.158 = f32[24,1,128,4,1,1,128]{6,5,4,3,2,1,0:T(1,128)} copy(f32[24,1,128,4,1,1,128]{6,2,3,0,5,4,1:T(8,128)S(1)} %fusion.1) | data formatting | bytes 12582912
  (186 shorter events, 31.9 us)
Async XLA Ops:
  8.1 114.5 %collective-permute-start.1 = (f32[8,8,512]{2,1,0:T(8,128)S(1)}, f32[8,8,512]{2,1,0:T(8,128)S(1)}, u32[]{:S(2)}, u32[]{:S(2)}) collective-permute-start(f32[8,8,512]{2,1,0:T(8,128)S(1)} %slice_bitcast_fusion.1), channel_id=1, source_target_pairs={{1,8},{2,16},{3,24},{4,32},{5,40},{6,48},{7,56},{8,1},{10,17},{11,... | collective-permute-start | bytes 393224 | tf_op jit(solution)/shard_map/ppermute | solution.py:116
  15.8 127.4 %collective-permute-start = (f32[8,128,512]{2,1,0:T(8,128)}, f32[8,128,512]{2,1,0:T(8,128)}, u32[]{:S(2)}, u32[]{:S(2)}) collective-permute-start(f32[8,128,512]{2,1,0:T(8,128)} %slice_bitcast_fusion), channel_id=1, source_target_pairs={{1,8},{2,16},{3,24},{4,32},{5,40},{6,48},{7,56},{8,1},{10,17},{11,... | collective-permute-start | bytes 6291464 | tf_op jit(solution)/shard_map/ppermute | solution.py:96
  23.3 11.0 %copy-start.9 = (s32[2,128]{1,0:T(2,128)S(1)}, s32[2,128]{1,0:T(2,128)}, u32[]{:S(2)}) copy-start(s32[2,128]{1,0:T(2,128)} %param.14) | copy-start | bytes 3076
  23.4 12.5 %copy-start.6 = (f32[1,512,512]{2,1,0:T(8,128)S(1)}, f32[1,512,512]{2,1,0:T(8,128)}, u32[]{:S(2)}) copy-start(f32[1,512,512]{2,1,0:T(8,128)} %param.9) | copy-start | bytes 3145732
  23.4 172.6 %all-to-all-start = ((f32[16,24,8,512]{3,2,1,0:T(8,128)}), f32[16,24,8,512]{3,2,1,0:T(8,128)}, u32[]{:S(2)}, u32[]{:S(2)}) async-start(f32[16,24,8,512]{3,2,1,0:T(8,128)} %stack.3), calls=%async_computation | async-start | bytes 12582912 | tf_op jit(solution)/shard_map/all_to_all | solution.py:101
  33.8 159.9 %all-gather.2.cloned.1.call-start = ((), (), s32[]{:S(2)}) async-start(), calls=%async_computation.2 | async-start | bytes 2228224 | tf_op jit(solution)/shard_map/all_gather | solution.py:118
  135.1 8.1 %copy-start = (f32[1,16,1,128,512]{4,3,2,1,0:T(8,128)S(1)}, f32[1,16,1,128,512]{4,3,2,1,0:T(8,128)}, u32[]{:S(2)}) copy-start(f32[1,16,1,128,512]{4,3,2,1,0:T(8,128)} %param.10) | copy-start | bytes 12582916
  137.3 10.1 %slice-start.2 = ((s8[8388608]{0:T(1024)(128)(4,1)}), s8[4194304]{0:T(1024)(128)(4,1)S(1)}, s32[]{:S(2)}) async-start(s8[8388608]{0:T(1024)(128)(4,1)} %bitcast.252), calls=%async_computation.5 | async-start | bytes 8388608
  143.2 4.1 slice-start.3
  202.5 25.5 %copy-start.2 = (f32[512,512]{1,0:T(8,128)S(1)}, f32[512,512]{1,0:T(8,128)}, u32[]{:S(2)}) copy-start(f32[512,512]{1,0:T(8,128)} %param.12) | copy-start | bytes 3145732
  202.5 299.3 %all-to-all-start.1 = ((f32[128,2,128,128]{3,2,1,0:T(8,128)}), f32[128,2,128,128]{3,2,1,0:T(8,128)}, u32[]{:S(2)}, u32[]{:S(2)}) async-start(f32[128,2,128,128]{3,2,1,0:T(8,128)} %bitcast.243), calls=%async_computation.1 | async-start | bytes 33554432 | tf_op jit(solution)/shard_map/all_to_all | solution.py:186
  228.4 108.5 %slice-start = ((s8[6291456]{0:T(1024)(128)(4,1)}), s8[2097152]{0:T(1024)(128)(4,1)S(1)}, s32[]{:S(2)}) async-start(s8[6291456]{0:T(1024)(128)(4,1)} %bitcast.245), calls=%async_computation.3 | async-start | bytes 4194304
  253.6 0.8 copy-start.1
  330.0 6.9 %slice-start.1 = ((s8[6291456]{0:T(1024)(128)(4,1)}), s8[4194304]{0:T(1024)(128)(4,1)S(1)}, s32[]{:S(2)}) async-start(s8[6291456]{0:T(1024)(128)(4,1)} %bitcast.245), calls=%async_computation.4 | async-start | bytes 8388608
  330.6 17.8 %copy-start.4 = (f32[256,256]{1,0:T(8,128)}, f32[256,256]{1,0:T(8,128)S(1)}, u32[]{:S(2)}) copy-start(f32[256,256]{1,0:T(8,128)S(1)} %select_maximum_fusion.7) | copy-start | bytes 786436
  360.5 7.8 %copy-start.7 = (f32[512,128]{1,0:T(8,128)S(1)}, f32[512,128]{1,0:T(8,128)}, u32[]{:S(2)}) copy-start(f32[512,128]{1,0:T(8,128)} %get-tuple-element.55) | copy-start | bytes 786436
  360.5 7.8 %copy-start.8 = (f32[128,128]{1,0:T(8,128)S(1)}, f32[128,128]{1,0:T(8,128)}, u32[]{:S(2)}) copy-start(f32[128,128]{1,0:T(8,128)} %get-tuple-element.32) | copy-start | bytes 196612
  360.5 8.9 %copy-start.3 = (f32[24,1,1,1,8,512]{5,4,3,2,1,0:T(8,128)S(1)}, f32[24,1,1,1,8,512]{5,4,3,2,1,0:T(8,128)}, u32[]{:S(2)}) copy-start(f32[24,1,1,1,8,512]{5,4,3,2,1,0:T(8,128)} %param.13) | copy-start | bytes 1179652
  360.5 8.9 %copy-start.5 = (f32[256,256]{1,0:T(8,128)S(1)}, f32[256,256]{1,0:T(8,128)}, u32[]{:S(2)}) copy-start(f32[256,256]{1,0:T(8,128)} %copy-done.4) | copy-start | bytes 786436
Sparse Core Ops, SparseCore 0:
  124.3 69.3 all-gather.1
